TPU v7x, 512 devices: a whole 4x4x16 slice. The times are simulated.
512 devices in a mesh: gx: 64 (over z, y_lo, core), gz: 8 (over x, y_hi).
Axes of the slice: x: 4, y: 4 (y_hi: 2, y_lo: 2; y = y_hi * 2 + y_lo), z: 16, core: 2. Of those that a mesh axis runs over, the one named last changes fastest.
Arguments:
- adjoint: bfloat16 [3, 512, 256, 256], P(None, 'gx', 'gz'), may hold values from -6 to 6
- strain: bfloat16 [512, 256, 256], P('gx', 'gz'), may hold values from -16 to 16
- correction: float32 [256, 256], P('gz'), may hold values from 0.3 to 3
- metric: float32 [256], replicated, may hold values from 0.5 to 4
- stream_inverse: bfloat16 [512, 512], replicated, may hold values from -0.081 to 1.081
- span_inverse: bfloat16 [256, 256], replicated, may hold values from -0.081 to 1.081
- wall_operator: bfloat16 [256, 256], replicated, may hold values from -0.081 to 1.081
Outputs:
- adjoint_next: bfloat16 [3, 512, 256, 256], P(None, 'gx', 'gz')
- gradient: float32 [256, 256], P('gz', 'gx')
All inputs are finite; a program needn't handle non-finite values.
Results may differ from a plain program's by a relative error of at most 0.013.
Values may be sent and summed in bfloat16 or wider, within the bound.
No kernel may reach another device: no remote copies, remote signals or barrier semaphores. Data moves between devices by JAX's collectives and lax.ppermute only.
A program may use at most 64 MiB of HBM per device.

v0:
```python
import jax
import jax.numpy as jnp
from jax import lax
from jax.sharding import PartitionSpec as P

near_coef = 7.0 / 9.0
far_coef = 1.0 / 36.0
time_step = 0.25
f32 = jnp.float32
bf16 = jnp.bfloat16


def stencil(source, axis):
    widened = source.astype(f32)
    near_diff = jnp.roll(widened, -1, axis) - jnp.roll(widened, 1, axis)
    far_diff = jnp.roll(widened, -2, axis) - jnp.roll(widened, 2, axis)
    return (near_coef * near_diff + far_coef * far_diff).astype(bf16)


def derivative(pencil, operator):
    right_side = stencil(pencil, 1)
    product = jnp.einsum("ij,cjp->cip", operator, right_side, preferred_element_type=f32)
    return product.astype(bf16)


def xor_order(blocks, mine):
    size = blocks.shape[0]
    bit = 1
    while bit < size:
        swapped = blocks.reshape(size // (2 * bit), 2, bit, *blocks.shape[1:])[:, ::-1]
        blocks = jnp.where(mine // bit % 2 == 1, swapped.reshape(blocks.shape), blocks)
        bit *= 2
    return blocks


def butterfly(blocks, mine):
    size = blocks.shape[0]
    blocks = xor_order(blocks, mine)
    bit = 1
    while bit < size:
        split = blocks.reshape(size // (2 * bit), 2, bit, *blocks.shape[1:])
        pairs = [(src, src ^ bit) for src in range(size)]
        moved = lax.ppermute(split[:, 1], "gz", pairs)
        blocks = jnp.stack([split[:, 0], moved], axis=1).reshape(blocks.shape)
        bit *= 2
    return xor_order(blocks, mine)


def split_wide(value):
    high = lax.reduce_precision(value, exponent_bits=8, mantissa_bits=7)
    return jnp.stack([high.astype(bf16), (value - high).astype(bf16)])


def join_wide(parts):
    return parts[0].astype(f32) + parts[1].astype(f32)


def row_derivative(pencil, operator):
    right_side = stencil(pencil, 0)
    return jnp.dot(operator, right_side, preferred_element_type=f32).astype(bf16)


def wall_derivative(source, wall_operator, metric):
    product = jnp.einsum("kxzj,ij->kxzi", source, wall_operator, preferred_element_type=f32)
    return product * metric


def on_device(adjoint, strain, correction, metric, stream_inverse, span_inverse, wall_operator):
    comps, nxl, nzl, ny = adjoint.shape
    gxn = lax.axis_size("gx")
    lanes = nzl * ny // gxn
    yparts = ny // lanes
    nx = nxl * gxn
    strain_wide = strain.astype(f32)
    viscosity = (correction[None] * strain_wide).astype(bf16)
    viscous = viscosity.astype(f32)
    xs = jnp.concatenate([adjoint, strain[None]], axis=0)
    xs = xs.reshape(comps + 1, nxl, nzl, yparts, lanes).transpose(2, 3, 1, 0, 4)
    xs = xs.reshape(gxn, nxl, (comps + 1) * lanes)
    xt = lax.all_to_all(xs, "gx", 0, 0, tiled=True).reshape(nx, (comps + 1) * lanes)
    stream_strain = xt[:, comps * lanes :].astype(f32)
    me = lax.axis_index("gx")
    z_at, y_at = (me // yparts, me % yparts)
    corr_row = lax.dynamic_slice(correction, (z_at, y_at * lanes), (1, lanes))
    stream_visc = (corr_row * stream_strain).astype(bf16).astype(f32)
    stream_visc = jnp.tile(stream_visc, (1, comps))
    stream_grad = row_derivative(xt[:, : comps * lanes], stream_inverse)
    stream_flux = (stream_visc * stream_grad.astype(f32)).astype(bf16)
    stream_div = row_derivative(stream_flux, stream_inverse)
    stream_sq = (stream_grad.astype(f32) ** 2).reshape(nx, comps, lanes).sum(axis=1)
    stream_sq = jnp.sum(stream_strain * stream_sq, axis=0)
    z_ids = lax.broadcasted_iota(jnp.int32, (nzl, yparts, lanes), 0)
    y_ids = lax.broadcasted_iota(jnp.int32, (nzl, yparts, lanes), 1)
    owned = (z_ids == z_at) & (y_ids == y_at)
    stream_part = jnp.where(owned, stream_sq[None, None], 0.0).reshape(nzl, ny)
    gzn = lax.axis_size("gz")
    mine = lax.axis_index("gz")
    zs = jnp.concatenate([adjoint, viscosity[None], strain[None]], axis=0)
    zt = lax.all_to_all(zs, "gz", 1, 2, tiled=True)[:, 0]
    span_visc = zt[comps].astype(f32)
    span_strain = zt[comps + 1].astype(f32)
    span_grad = derivative(zt[:comps], span_inverse)
    span_flux = (span_visc[None] * span_grad.astype(f32)).astype(bf16)
    span_div = derivative(span_flux, span_inverse)
    span_sq = jnp.sum(span_strain[None] * span_grad.astype(f32) ** 2, axis=0)
    span_back = jnp.concatenate([span_div, split_wide(span_sq)], axis=0)
    span_back = span_back.reshape(span_back.shape[0], gzn, nzl, ny).transpose(1, 0, 2, 3)
    span_out = butterfly(span_back, mine)
    span_part = jnp.sum(join_wide(span_out[:, comps:].transpose(1, 0, 2, 3)), axis=0)
    span_div = span_out[:, :comps].transpose(1, 0, 2, 3)
    wall_grad = wall_derivative(adjoint, wall_operator, metric).astype(bf16)
    wall_flux = (viscous[None] * wall_grad.astype(f32)).astype(bf16)
    wall_div = wall_derivative(wall_flux, wall_operator, metric)
    wall_part = jnp.sum(strain_wide[None] * wall_grad.astype(f32) ** 2, axis=(0, 1))
    partial_sum = stream_part + span_part + wall_part
    pieces = split_wide(partial_sum.T.reshape(gxn, -1))
    extra = jnp.zeros((gxn, nxl - 2, lanes), bf16)
    extra = jnp.concatenate([pieces[0][:, None], pieces[1][:, None], extra], axis=1)
    back = jnp.concatenate([stream_div.reshape(gxn, nxl, comps * lanes), extra], axis=2)
    back = lax.all_to_all(back, "gx", 0, 0, tiled=True)
    summed = jnp.sum(join_wide(back[:, :2, comps * lanes :].transpose(1, 0, 2)), axis=0)
    summed = summed.reshape(ny // gxn, nzl).T
    back = back[:, :, : comps * lanes].reshape(nzl, yparts, nxl, comps, lanes)
    stream_div = back.transpose(3, 2, 0, 1, 4).reshape(comps, nxl, nzl, ny)
    total = stream_div.astype(f32) + wall_div
    total = total + span_div.astype(f32)
    updated = (adjoint.astype(f32) + time_step * total).astype(bf16)
    gradient = -summed / nx
    return (updated, gradient)


def solution(mesh):
    in_specs = (P(None, "gx", "gz", None), P("gx", "gz", None), P("gz", None), P(), P(), P(), P())
    out_specs = (P(None, "gx", "gz", None), P("gz", "gx"))
    return jax.shard_map(
        on_device, mesh=mesh, in_specs=in_specs, out_specs=out_specs, check_vma=False
    )
```

profile of v0, /device:TPU:8, one launch (start us, length us, event | category | flops | bytes accessed | tf_op | source)
XLA Modules:
  0.0 143.3 jit_solution(535685703489380704)
XLA Ops:
  0.7 1.7 %fusion.47 = (f32[8,32,256]{2,1,0:T(8,128)}, bf16[1,8,32,256]{3,2,0,1:T(8,128)(2,1)S(1)}) fusion(bf16[8,32,256]{2,1,0:T(8,128)(2,1)} %param.8, f32[32,256]{1,0:T(8,128)} %param.9), kind=kLoop, calls=%fused_computation.92 | loop fusion | flops 262144 | bytes 557056 | tf_op jit(solution)/shard_map/convert_element_type | solution.py:76
  2.4 1.8 %pad_maximum_fusion = bf16[5,8,32,256]{3,2,0,1:T(8,128)(2,1)} fusion(bf16[1,8,32,256]{3,2,0,1:T(8,128)(2,1)} %bitcast.145, bf16[1,8,32,256]{3,2,0,1:T(8,128)(2,1)S(1)} %get-tuple-element.50, bf16[3,8,32,256]{3,2,1,0:T(8,128)(2,1)S(1)} %copy-done.1), kind=kLoop, calls=%fused_computation.49 | loop fusion | flops 1966080 | bytes 1310720 | tf_op jit(solution)/shard_map/concatenate | solution.py:98
  4.2 6.0 %all-to-all-start.1 = ((bf16[5,8,32,256]{3,2,0,1:T(8,128)(2,1)}), bf16[5,8,32,256]{3,2,0,1:T(8,128)(2,1)S(1)}, u32[]{:S(2)}, u32[]{:S(2)}) async-start(bf16[5,8,32,256]{3,2,0,1:T(8,128)(2,1)} %pad_maximum_fusion), calls=%async_computation.1 | async-start | bytes 1310720 | tf_op jit(solution)/shard_map/all_to_all | solution.py:99
  10.2 12.1 %all-to-all-done.1 = bf16[5,8,32,256]{3,2,0,1:T(8,128)(2,1)S(1)} async-done(((bf16[5,8,32,256]{3,2,0,1:T(8,128)(2,1)}), bf16[5,8,32,256]{3,2,0,1:T(8,128)(2,1)S(1)}, u32[]{:S(2)}, u32[]{:S(2)}) %all-to-all-start.1) | async-done | bytes 655392 | tf_op jit(solution)/shard_map/all_to_all | solution.py:99
  22.8 0.8 copy-done.6
  23.6 0.5 fusion.29
  24.4 0.5 convolution_convert_fusion
  25.5 3.6 %collective-permute-start = (bf16[4,1,5,32,256]{4,3,0,2,1:T(8,128)(2,1)S(1)}, bf16[4,1,5,32,256]{4,3,0,2,1:T(8,128)(2,1)S(1)}, u32[]{:S(2)}, u32[]{:S(2)}) collective-permute-start(bf16[4,1,5,32,256]{4,3,0,2,1:T(8,128)(2,1)S(1)} %get-tuple-element.36), channel_id=1, source_target_pairs={{0,1},{1,0},{2,3},{3,2},{4,5},{5,4},{6,7},{7,6},{8,9},{9,8},{10,11... | collective-permute-start | bytes 983048 | tf_op jit(solution)/shard_map/ppermute | solution.py:43
  29.3 0.5 copy.48
  29.9 0.8 pad_maximum_fusion.4
  30.8 17.3 %all-to-all-start = ((bf16[64,8,512]{2,1,0:T(8,128)(2,1)}), bf16[64,8,512]{2,1,0:T(8,128)(2,1)}, u32[]{:S(2)}, u32[]{:S(2)}) async-start(bf16[64,8,512]{2,1,0:T(8,128)(2,1)} %bitcast.2), calls=%async_computation | async-start | bytes 1048576 | tf_op jit(solution)/shard_map/all_to_all | solution.py:80
  48.3 2.5 %collective-permute-start.1 = (bf16[2,2,5,32,256]{4,3,1,2,0:T(8,128)(2,1)S(1)}, bf16[2,2,5,32,256]{4,3,1,2,0:T(8,128)(2,1)S(1)}, u32[]{:S(2)}, u32[]{:S(2)}) collective-permute-start(bf16[2,2,5,32,256]{4,3,1,2,0:T(8,128)(2,1)S(1)} %bitcast.154), channel_id=1, source_target_pairs={{0,2},{1,3},{2,0},{3,1},{4,6},{5,7},{6,4},{7,5},{8,10},{9,11},{10,... | collective-permute-start | bytes 983048 | tf_op jit(solution)/shard_map/ppermute | solution.py:43
  50.8 0.5 iota_compare_fusion.1
  51.3 0.6 broadcast_bitcast_fusion
  51.9 8.0 %collective-permute-done.1 = bf16[2,2,5,32,256]{4,3,1,2,0:T(8,128)(2,1)S(1)} collective-permute-done((bf16[2,2,5,32,256]{4,3,1,2,0:T(8,128)(2,1)S(1)}, bf16[2,2,5,32,256]{4,3,1,2,0:T(8,128)(2,1)S(1)}, u32[]{:S(2)}, u32[]{:S(2)}) %collective-permute-start.1) | collective-permute-done | bytes 327712 | tf_op jit(solution)/shard_map/ppermute | solution.py:43
  60.1 2.8 %collective-permute-start.2 = (bf16[1,4,5,32,256]{4,3,1,2,0:T(8,128)(2,1)S(1)}, bf16[1,4,5,32,256]{4,3,1,2,0:T(8,128)(2,1)S(1)}, u32[]{:S(2)}, u32[]{:S(2)}) collective-permute-start(bf16[1,4,5,32,256]{4,3,1,2,0:T(8,128)(2,1)S(1)} %get-tuple-element.32), channel_id=1, source_target_pairs={{0,4},{1,5},{2,6},{3,7},{4,0},{5,1},{6,2},{7,3},{8,12},{9,13},{10,... | collective-permute-start | bytes 983048 | tf_op jit(solution)/shard_map/ppermute | solution.py:43
  63.0 0.8 dynamic-slice_bitcast_fusion
  63.7 1.8 %multiply_reduce_fusion = (f32[32,256]{1,0:T(8,128)}, f32[3,8,32,256]{3,2,1,0:T(8,128)}) fusion(f32[8,32,256]{2,1,0:T(8,128)S(1)} %convert_element_type.211, f32[256]{0:T(256)S(1)} %copy-done.10, bf16[3,8,32,256]{3,2,1,0:T(8,128)(2,1)S(1)} %copy-done.1, bf16[256,256]{1,0:T(8,128)(2,1)S(1)} %copy-done.7), kind=kOutput, calls=%fused_computation.46 | convolution fusion | flops 101834752 | bytes 1606656 | tf_op jit(solution)/shard_map/kxzj,ij->kxzi/dot_general | solution.py:64
  65.5 7.0 %collective-permute-done.2 = bf16[1,4,5,32,256]{4,3,1,2,0:T(8,128)(2,1)S(1)} collective-permute-done((bf16[1,4,5,32,256]{4,3,1,2,0:T(8,128)(2,1)S(1)}, bf16[1,4,5,32,256]{4,3,1,2,0:T(8,128)(2,1)S(1)}, u32[]{:S(2)}, u32[]{:S(2)}) %collective-permute-start.2) | collective-permute-done | bytes 327712 | tf_op jit(solution)/shard_map/ppermute | solution.py:43
  72.6 1.0 maximum_select_fusion
  73.6 1.1 rev.22
  74.7 1.0 select_select_fusion.1
  75.7 1.1 rev.23
  76.8 1.0 select_select_fusion
  77.8 1.0 slice_bitcast_fusion.2
  78.8 0.6 add_reduce_fusion
  79.4 2.2 %all-to-all-done = bf16[64,8,512]{2,1,0:T(8,128)(2,1)} async-done(((bf16[64,8,512]{2,1,0:T(8,128)(2,1)}), bf16[64,8,512]{2,1,0:T(8,128)(2,1)}, u32[]{:S(2)}, u32[]{:S(2)}) %all-to-all-start) | async-done | bytes 524320 | tf_op jit(solution)/shard_map/all_to_all | solution.py:80
  81.6 0.9 slice.224
  82.5 1.0 slice.225
  83.5 0.2 copy.68
  83.7 0.2 fusion.80
  84.0 1.4 fusion.82
  85.3 0.8 fusion.79
  86.1 0.8 fusion.81
  87.1 2.3 %fusion.30 = (f32[512,384]{0,1:T(8,128)S(1)}, f32[512,384]{0,1:T(8,128)S(1)}) fusion(f32[512,128]{0,1:T(8,128)S(1)} %fusion.42, bf16[512,512]{1,0:T(8,128)(2,1)S(1)} %copy-done, f32[1,384]{0,1:T(8,128)} %get-tuple-element.44, f32[511,384]{0,1:T(8,128)} %get-tuple-element.46, f32[511,384]{0,1:T(8,128)} %get-tuple-element.45, ...), kind=kOutput, calls=%fused_computation.64 | convolution fusion | flops 204472320 | bytes 5505024 | tf_op jit(solution)/shard_map/dot_general | solution.py:60
  89.5 0.3 fusion.67
  89.8 0.3 fusion.65
  90.3 0.7 fusion.11
  91.1 0.2 copy.52
  91.6 0.5 copy-done.8
  92.5 0.2 maximum_maximum_fusion
  92.7 44.8 %all_to_all.19 = bf16[64,8,512]{2,1,0:T(8,128)(2,1)S(1)} all-to-all(bf16[64,8,512]{2,1,0:T(8,128)(2,1)S(1)} %maximum_maximum_fusion), channel_id=1, replica_groups=mesh['gx'=64,'gz'=8] {'gx'}, dimensions={0} | all-to-all | bytes 1048576 | tf_op jit(solution)/shard_map/all_to_all | solution.py:120
  137.5 0.8 copy-done.4
  138.3 0.4 copy.76
  138.8 0.6 reshape.254
  139.4 0.9 slice_bitcast_fusion.3
  140.4 0.7 div.47
  141.1 2.2 %fusion.6 = bf16[3,8,32,256]{3,2,1,0:T(8,128)(2,1)} fusion(f32[3,8,32,256]{3,2,1,0:T(8,128)S(1)} %reshape.254, bf16[3,8,32,256]{3,2,1,0:T(8,128)(2,1)S(1)} %copy-done.1, f32[3,8,32,256]{3,2,1,0:T(8,128)S(1)} %copy-done.2, bf16[8,5,32,256]{3,2,0,1:T(8,128)(2,1)} %select_select_fusion, f32[8,32,256]{2,1,0:T(8,128)S(1)} %copy-done.5, f32[256]{0:T(256)S(1)} %copy-done.10, ...), kind=kOutput, calls=%fused_computation.8 | convolution fusion | flops 102629376 | bytes 3146752 | tf_op jit(solution)/shard_map/kxzj,ij->kxzi/dot_general | solution.py:64
  (75 shorter events, 3.1 us)
Async XLA Ops:
  0.6 86.5 %copy-start = (bf16[512,512]{1,0:T(8,128)(2,1)S(1)}, bf16[512,512]{1,0:T(8,128)(2,1)}, u32[]{:S(2)}) copy-start(bf16[512,512]{1,0:T(8,128)(2,1)} %param.11) | copy-start | bytes 1572868
  0.6 1.7 %copy-start.1 = (bf16[3,8,32,256]{3,2,1,0:T(8,128)(2,1)S(1)}, bf16[3,8,32,256]{3,2,1,0:T(8,128)(2,1)}, u32[]{:S(2)}) copy-start(bf16[3,8,32,256]{3,2,1,0:T(8,128)(2,1)} %param.7) | copy-start | bytes 1179652
  4.2 18.1 %all-to-all-start.1 = ((bf16[5,8,32,256]{3,2,0,1:T(8,128)(2,1)}), bf16[5,8,32,256]{3,2,0,1:T(8,128)(2,1)S(1)}, u32[]{:S(2)}, u32[]{:S(2)}) async-start(bf16[5,8,32,256]{3,2,0,1:T(8,128)(2,1)} %pad_maximum_fusion), calls=%async_computation.1 | async-start | bytes 1310720 | tf_op jit(solution)/shard_map/all_to_all | solution.py:99
  22.7 0.9 copy-start.6
  25.4 3.8 %copy-start.3 = (bf16[8,32,256]{2,1,0:T(8,128)(2,1)S(1)}, bf16[8,32,256]{2,1,0:T(8,128)(2,1)}, u32[]{:S(2)}) copy-start(bf16[8,32,256]{2,1,0:T(8,128)(2,1)} %param.8) | copy-start | bytes 393220
  25.5 22.7 %collective-permute-start = (bf16[4,1,5,32,256]{4,3,0,2,1:T(8,128)(2,1)S(1)}, bf16[4,1,5,32,256]{4,3,0,2,1:T(8,128)(2,1)S(1)}, u32[]{:S(2)}, u32[]{:S(2)}) collective-permute-start(bf16[4,1,5,32,256]{4,3,0,2,1:T(8,128)(2,1)S(1)} %get-tuple-element.36), channel_id=1, source_target_pairs={{0,1},{1,0},{2,3},{3,2},{4,5},{5,4},{6,7},{7,6},{8,9},{9,8},{10,11... | collective-permute-start | bytes 983048 | tf_op jit(solution)/shard_map/ppermute | solution.py:43
  30.8 50.8 %all-to-all-start = ((bf16[64,8,512]{2,1,0:T(8,128)(2,1)}), bf16[64,8,512]{2,1,0:T(8,128)(2,1)}, u32[]{:S(2)}, u32[]{:S(2)}) async-start(bf16[64,8,512]{2,1,0:T(8,128)(2,1)} %bitcast.2), calls=%async_computation | async-start | bytes 1048576 | tf_op jit(solution)/shard_map/all_to_all | solution.py:80
  48.3 11.6 %collective-permute-start.1 = (bf16[2,2,5,32,256]{4,3,1,2,0:T(8,128)(2,1)S(1)}, bf16[2,2,5,32,256]{4,3,1,2,0:T(8,128)(2,1)S(1)}, u32[]{:S(2)}, u32[]{:S(2)}) collective-permute-start(bf16[2,2,5,32,256]{4,3,1,2,0:T(8,128)(2,1)S(1)} %bitcast.154), channel_id=1, source_target_pairs={{0,2},{1,3},{2,0},{3,1},{4,6},{5,7},{6,4},{7,5},{8,10},{9,11},{10,... | collective-permute-start | bytes 983048 | tf_op jit(solution)/shard_map/ppermute | solution.py:43
  60.0 3.7 %copy-start.7 = (bf16[256,256]{1,0:T(8,128)(2,1)S(1)}, bf16[256,256]{1,0:T(8,128)(2,1)}, u32[]{:S(2)}) copy-start(bf16[256,256]{1,0:T(8,128)(2,1)} %param.13) | copy-start | bytes 393220
  60.0 3.7 %copy-start.10 = (f32[256]{0:T(256)S(1)}, f32[256]{0:T(256)}, u32[]{:S(2)}) copy-start(f32[256]{0:T(256)} %param.10) | copy-start | bytes 3076
  60.1 12.4 %collective-permute-start.2 = (bf16[1,4,5,32,256]{4,3,1,2,0:T(8,128)(2,1)S(1)}, bf16[1,4,5,32,256]{4,3,1,2,0:T(8,128)(2,1)S(1)}, u32[]{:S(2)}, u32[]{:S(2)}) collective-permute-start(bf16[1,4,5,32,256]{4,3,1,2,0:T(8,128)(2,1)S(1)} %get-tuple-element.32), channel_id=1, source_target_pairs={{0,4},{1,5},{2,6},{3,7},{4,0},{5,1},{6,2},{7,3},{8,12},{9,13},{10,... | collective-permute-start | bytes 983048 | tf_op jit(solution)/shard_map/ppermute | solution.py:43
  91.3 0.8 copy-start.8
  91.3 0.8 copy-start.9
  91.3 0.8 copy-start.11
  91.4 0.8 copy-start.12
  137.5 0.8 copy-start.4
  138.7 2.3 %copy-start.2 = (f32[3,8,32,256]{3,2,1,0:T(8,128)S(1)}, f32[3,8,32,256]{3,2,1,0:T(8,128)}, u32[]{:S(2)}) copy-start(f32[3,8,32,256]{3,2,1,0:T(8,128)} %get-tuple-element.54) | copy-start | bytes 2359300
  138.7 2.3 %copy-start.5 = (f32[8,32,256]{2,1,0:T(8,128)S(1)}, f32[8,32,256]{2,1,0:T(8,128)}, u32[]{:S(2)}) copy-start(f32[8,32,256]{2,1,0:T(8,128)} %get-tuple-element.49) | copy-start | bytes 786436
where the time goes:
time: 144 us; the launch traced here: 143 us
  blocking collectives  44.8 us (31%)
  starting transfers between devices  32.2 us (22%)
  waiting for transfers between devices  29.3 us (20%)
  local copies, waits for them, and re-layouts  17.9 us (12%)
  other arithmetic  9.69 us (7%)
  matrix products  8.05 us (6%)
    all_to_all x1, blocking collectives, on_device(): back = lax.all_to_all(back, 'gx', 0, 0, tiled=True)  44.8 us
    all_to_all x1, starting transfers between devices, on_device(): lax.all_to_all(xs, 'gx', 0, 0, tiled=True).reshape(nx, (comps + 1) * lanes)  17.3 us
    ppermute x3, waiting for transfers between devices, butterfly(): moved = lax.ppermute(split[:, 1], 'gz', pairs)  15 us
    all_to_all x1, waiting for transfers between devices, on_device(): zt = lax.all_to_all(zs, 'gz', 1, 2, tiled=True)[:, 0]  12.1 us
    ppermute x3, starting transfers between devices, butterfly(): moved = lax.ppermute(split[:, 1], 'gz', pairs)  8.91 us
    all_to_all x1, starting transfers between devices, on_device(): zt = lax.all_to_all(zs, 'gz', 1, 2, tiled=True)[:, 0]  6.03 us
    dot_general x2, matrix products, wall_derivative(): jnp.einsum('kxzj,ij->kxzi', source, wall_operator, preferred_element_type...  4.02 us
    select_n x6, other arithmetic, xor_order(): jnp.where(mine // bit % 2 == 1, swapped.reshape(blocks.shape), blocks)  3.1 us
  transfers between devices with their start and end apart: 5, of which 4 were waited for; matrix products, arithmetic and copies ran while one was open for 9% of the time, Pallas kernels for 0%

commit v1 on v0

--- a/solution.py
+++ b/solution.py
@@ -96,7 +96,9 @@
     gzn = lax.axis_size("gz")
     mine = lax.axis_index("gz")
     zs = jnp.concatenate([adjoint, viscosity[None], strain[None]], axis=0)
-    zt = lax.all_to_all(zs, "gz", 1, 2, tiled=True)[:, 0]
+    zt = jnp.concatenate(
+        lax.all_to_all(jnp.stack(jnp.split(zs, lax.axis_size("gz"), axis=1)), "gz", 0, 0), axis=2
+    )[:, 0]
     span_visc = zt[comps].astype(f32)
     span_strain = zt[comps + 1].astype(f32)
     span_grad = derivative(zt[:comps], span_inverse)

time: 144 us -> 149 us (1.035)
  local copies, waits for them, and re-layouts: 17.9 us -> 24.8 us
  other arithmetic: 9.69 us -> 8.02 us
    unnamed x30 -> x43, local copies, waits for them, and re-layouts: 2.52 us -> 8.04 us
    concatenate x1, other arithmetic: 1.78 us -> 0.08 us  [on_device(): zs = jnp.concatenate([adjoint, viscosity[None], strain[None]], axis=0)]
  transfers between devices with their start and end apart: 5 -> 5, of which waited for: 4 -> 4; matrix products, arithmetic and copies ran while one was open for 9% -> 8% of each run, Pallas kernels for 0% -> 0%
where the time goes in v1:
time: 149 us; the launch traced here: 148 us
  blocking collectives  44.7 us (30%)
  starting transfers between devices  32.2 us (22%)
  waiting for transfers between devices  29.2 us (20%)
  local copies, waits for them, and re-layouts  24.8 us (17%)
  other arithmetic  8.02 us (5%)
  matrix products  7.89 us (5%)
    all_to_all x1, blocking collectives, on_device(): back = lax.all_to_all(back, 'gx', 0, 0, tiled=True)  44.7 us
    all_to_all x1, starting transfers between devices, on_device(): lax.all_to_all(xs, 'gx', 0, 0, tiled=True).reshape(nx, (comps + 1) * lanes)  17.3 us
    ppermute x3, waiting for transfers between devices, butterfly(): moved = lax.ppermute(split[:, 1], 'gz', pairs)  14.9 us
    all_to_all x1, waiting for transfers between devices, on_device(): lax.all_to_all(jnp.stack(jnp.split(zs, lax.axis_size('gz'), axis=1)), 'gz...  12.1 us
    ppermute x3, starting transfers between devices, butterfly(): moved = lax.ppermute(split[:, 1], 'gz', pairs)  8.91 us
    unnamed x43, local copies, waits for them, and re-layouts  8.04 us
    all_to_all x1, starting transfers between devices, on_device(): lax.all_to_all(jnp.stack(jnp.split(zs, lax.axis_size('gz'), axis=1)), 'gz...  6.03 us
    dot_general x2, matrix products, wall_derivative(): jnp.einsum('kxzj,ij->kxzi', source, wall_operator, preferred_element_type...  3.97 us
  transfers between devices with their start and end apart: 5, of which 4 were waited for; matrix products, arithmetic and copies ran while one was open for 8% of the time, Pallas kernels for 0%

profile of v1, /device:TPU:8, one launch (start us, length us, event | category | flops | bytes accessed | tf_op | source)
XLA Modules:
  0.0 148.3 jit_solution(3952512014182737671)
XLA Ops:
  0.7 1.7 %fusion.55 = (f32[8,32,256]{2,1,0:T(8,128)}, bf16[1,8,32,256]{3,2,1,0:T(8,128)(2,1)S(1)}) fusion(bf16[8,32,256]{2,1,0:T(8,128)(2,1)} %param.8, f32[32,256]{1,0:T(8,128)} %param.9), kind=kLoop, calls=%fused_computation.108 | loop fusion | flops 262144 | bytes 557056 | tf_op jit(solution)/shard_map/convert_element_type | solution.py:76
  2.5 0.6 fusion.54
  3.1 0.6 fusion.53
  3.7 0.7 fusion.52
  4.4 0.7 fusion.51
  5.1 0.6 fusion.50
  5.7 0.6 fusion.49
  6.3 0.6 fusion.48
  6.9 0.6 fusion.47
  7.6 6.0 %all-to-all-start.1 = ((bf16[8,5,1,32,256]{4,3,1,2,0:T(8,128)(2,1)}), bf16[8,5,1,32,256]{4,3,1,2,0:T(8,128)(2,1)S(1)}, u32[]{:S(2)}, u32[]{:S(2)}) async-start(bf16[8,5,1,32,256]{4,3,1,2,0:T(8,128)(2,1)} %fusion.47), calls=%async_computation.1 | async-start | bytes 1310720 | tf_op jit(solution)/shard_map/all_to_all | solution.py:100
  13.6 12.1 %all-to-all-done.1 = bf16[8,5,1,32,256]{4,3,1,2,0:T(8,128)(2,1)S(1)} async-done(((bf16[8,5,1,32,256]{4,3,1,2,0:T(8,128)(2,1)}), bf16[8,5,1,32,256]{4,3,1,2,0:T(8,128)(2,1)S(1)}, u32[]{:S(2)}, u32[]{:S(2)}) %all-to-all-start.1) | async-done | bytes 655392 | tf_op jit(solution)/shard_map/all_to_all | solution.py:100
  26.3 0.8 copy-done.8
  27.1 0.5 fusion.29
  28.9 0.8 fusion.85
  29.7 3.6 %collective-permute-start = (bf16[4,1,5,32,256]{4,3,0,2,1:T(8,128)(2,1)}, bf16[4,1,5,32,256]{4,3,0,2,1:T(8,128)(2,1)S(1)}, u32[]{:S(2)}, u32[]{:S(2)}) collective-permute-start(bf16[4,1,5,32,256]{4,3,0,2,1:T(8,128)(2,1)} %get-tuple-element.36), channel_id=1, source_target_pairs={{0,1},{1,0},{2,3},{3,2},{4,5},{5,4},{6,7},{7,6},{8,9},{9,8},{10,11... | collective-permute-start | bytes 983048 | tf_op jit(solution)/shard_map/ppermute | solution.py:43
  34.1 0.9 pad_maximum_fusion.4
  34.9 17.3 %all-to-all-start = ((bf16[64,8,512]{2,1,0:T(8,128)(2,1)}), bf16[64,8,512]{2,1,0:T(8,128)(2,1)}, u32[]{:S(2)}, u32[]{:S(2)}) async-start(bf16[64,8,512]{2,1,0:T(8,128)(2,1)} %bitcast.2), calls=%async_computation | async-start | bytes 1048576 | tf_op jit(solution)/shard_map/all_to_all | solution.py:80
  52.5 2.5 %collective-permute-start.1 = (bf16[2,2,5,32,256]{4,3,1,2,0:T(8,128)(2,1)S(1)}, bf16[2,2,5,32,256]{4,3,1,2,0:T(8,128)(2,1)S(1)}, u32[]{:S(2)}, u32[]{:S(2)}) collective-permute-start(bf16[2,2,5,32,256]{4,3,1,2,0:T(8,128)(2,1)S(1)} %bitcast.203), channel_id=1, source_target_pairs={{0,2},{1,3},{2,0},{3,1},{4,6},{5,7},{6,4},{7,5},{8,10},{9,11},{10,... | collective-permute-start | bytes 983048 | tf_op jit(solution)/shard_map/ppermute | solution.py:43
  55.0 0.6 iota_compare_fusion.1
  55.5 0.6 broadcast_bitcast_fusion
  56.1 7.9 %collective-permute-done.1 = bf16[2,2,5,32,256]{4,3,1,2,0:T(8,128)(2,1)S(1)} collective-permute-done((bf16[2,2,5,32,256]{4,3,1,2,0:T(8,128)(2,1)S(1)}, bf16[2,2,5,32,256]{4,3,1,2,0:T(8,128)(2,1)S(1)}, u32[]{:S(2)}, u32[]{:S(2)}) %collective-permute-start.1) | collective-permute-done | bytes 327712 | tf_op jit(solution)/shard_map/ppermute | solution.py:43
  64.3 2.8 %collective-permute-start.2 = (bf16[1,4,5,32,256]{4,3,1,2,0:T(8,128)(2,1)S(1)}, bf16[1,4,5,32,256]{4,3,1,2,0:T(8,128)(2,1)S(1)}, u32[]{:S(2)}, u32[]{:S(2)}) collective-permute-start(bf16[1,4,5,32,256]{4,3,1,2,0:T(8,128)(2,1)S(1)} %get-tuple-element.32), channel_id=1, source_target_pairs={{0,4},{1,5},{2,6},{3,7},{4,0},{5,1},{6,2},{7,3},{8,12},{9,13},{10,... | collective-permute-start | bytes 983048 | tf_op jit(solution)/shard_map/ppermute | solution.py:43
  67.1 0.8 dynamic-slice_bitcast_fusion
  67.9 1.8 %multiply_reduce_fusion = (f32[32,256]{1,0:T(8,128)}, f32[3,8,32,256]{3,2,1,0:T(8,128)}) fusion(f32[8,32,256]{2,1,0:T(8,128)S(1)} %convert_element_type.211, f32[256]{0:T(256)S(1)} %copy-done.13, bf16[3,8,32,256]{3,2,1,0:T(8,128)(2,1)S(1)} %copy-done.1, bf16[256,256]{1,0:T(8,128)(2,1)S(1)} %copy-done.9), kind=kOutput, calls=%fused_computation.46 | convolution fusion | flops 101834752 | bytes 1606656 | tf_op jit(solution)/shard_map/kxzj,ij->kxzi/dot_general | solution.py:64
  69.7 7.0 %collective-permute-done.2 = bf16[1,4,5,32,256]{4,3,1,2,0:T(8,128)(2,1)S(1)} collective-permute-done((bf16[1,4,5,32,256]{4,3,1,2,0:T(8,128)(2,1)S(1)}, bf16[1,4,5,32,256]{4,3,1,2,0:T(8,128)(2,1)S(1)}, u32[]{:S(2)}, u32[]{:S(2)}) %collective-permute-start.2) | collective-permute-done | bytes 327712 | tf_op jit(solution)/shard_map/ppermute | solution.py:43
  76.8 0.9 maximum_select_fusion
  77.7 1.1 rev.22
  78.9 0.9 select_select_fusion.1
  79.8 1.1 rev.23
  80.9 1.0 select_select_fusion
  81.9 1.0 slice_bitcast_fusion.2
  82.9 0.6 add_reduce_fusion
  83.5 2.2 %all-to-all-done = bf16[64,8,512]{2,1,0:T(8,128)(2,1)} async-done(((bf16[64,8,512]{2,1,0:T(8,128)(2,1)}), bf16[64,8,512]{2,1,0:T(8,128)(2,1)}, u32[]{:S(2)}, u32[]{:S(2)}) %all-to-all-start) | async-done | bytes 524320 | tf_op jit(solution)/shard_map/all_to_all | solution.py:80
  85.7 0.9 slice.223
  86.6 1.0 slice.224
  88.1 1.4 fusion.90
  89.5 0.8 fusion.87
  90.3 0.8 fusion.89
  91.3 0.8 copy-done.6
  92.2 2.2 %fusion.30 = (f32[512,384]{0,1:T(8,128)S(1)}, f32[512,384]{0,1:T(8,128)S(1)}) fusion(f32[512,128]{0,1:T(8,128)S(1)} %fusion.42, bf16[512,512]{1,0:T(8,128)(2,1)S(1)} %copy-done, f32[1,384]{0,1:T(8,128)} %get-tuple-element.44, f32[511,384]{0,1:T(8,128)} %get-tuple-element.46, f32[511,384]{0,1:T(8,128)} %get-tuple-element.45, ...), kind=kOutput, calls=%fused_computation.64 | convolution fusion | flops 204472320 | bytes 5505024 | tf_op jit(solution)/shard_map/dot_general | solution.py:60
  95.3 0.7 fusion.11
  96.5 0.6 copy-done.11
  97.7 44.7 %all_to_all.15 = bf16[64,8,512]{2,1,0:T(8,128)(2,1)S(1)} all-to-all(bf16[64,8,512]{2,1,0:T(8,128)(2,1)S(1)} %maximum_maximum_fusion), channel_id=1, replica_groups=mesh['gx'=64,'gz'=8] {'gx'}, dimensions={0} | all-to-all | bytes 1048576 | tf_op jit(solution)/shard_map/all_to_all | solution.py:122
  142.5 0.8 copy-done.4
  143.7 0.6 reshape.252
  144.4 1.0 slice_bitcast_fusion.11
  145.4 0.7 div.47
  146.1 2.1 %fusion.6 = bf16[3,8,32,256]{3,2,1,0:T(8,128)(2,1)} fusion(f32[3,8,32,256]{3,2,1,0:T(8,128)S(1)} %reshape.252, bf16[3,8,32,256]{3,2,1,0:T(8,128)(2,1)S(1)} %copy-done.1, f32[3,8,32,256]{3,2,1,0:T(8,128)S(1)} %copy-done.2, bf16[8,5,32,256]{3,2,0,1:T(8,128)(2,1)} %select_select_fusion, f32[8,32,256]{2,1,0:T(8,128)S(1)} %copy-done.5, f32[256]{0:T(256)S(1)} %copy-done.13, ...), kind=kOutput, calls=%fused_computation.8 | convolution fusion | flops 102629376 | bytes 3146752 | tf_op jit(solution)/shard_map/kxzj,ij->kxzi/dot_general | solution.py:64
  (89 shorter events, 6.1 us)
Async XLA Ops:
  0.6 90.7 %copy-start = (bf16[512,512]{1,0:T(8,128)(2,1)S(1)}, bf16[512,512]{1,0:T(8,128)(2,1)}, u32[]{:S(2)}) copy-start(bf16[512,512]{1,0:T(8,128)(2,1)} %param.11) | copy-start | bytes 1572868
  0.6 1.7 %copy-start.3 = (bf16[8,32,256]{2,1,0:T(8,128)(2,1)S(1)}, bf16[8,32,256]{2,1,0:T(8,128)(2,1)}, u32[]{:S(2)}) copy-start(bf16[8,32,256]{2,1,0:T(8,128)(2,1)} %param.8) | copy-start | bytes 393220
  0.7 1.7 %copy-start.1 = (bf16[3,8,32,256]{3,2,1,0:T(8,128)(2,1)S(1)}, bf16[3,8,32,256]{3,2,1,0:T(8,128)(2,1)}, u32[]{:S(2)}) copy-start(bf16[3,8,32,256]{3,2,1,0:T(8,128)(2,1)} %param.7) | copy-start | bytes 1179652
  7.6 18.1 %all-to-all-start.1 = ((bf16[8,5,1,32,256]{4,3,1,2,0:T(8,128)(2,1)}), bf16[8,5,1,32,256]{4,3,1,2,0:T(8,128)(2,1)S(1)}, u32[]{:S(2)}, u32[]{:S(2)}) async-start(bf16[8,5,1,32,256]{4,3,1,2,0:T(8,128)(2,1)} %fusion.47), calls=%async_computation.1 | async-start | bytes 1310720 | tf_op jit(solution)/shard_map/all_to_all | solution.py:100
  26.2 0.9 copy-start.8
  29.7 22.7 %collective-permute-start = (bf16[4,1,5,32,256]{4,3,0,2,1:T(8,128)(2,1)}, bf16[4,1,5,32,256]{4,3,0,2,1:T(8,128)(2,1)S(1)}, u32[]{:S(2)}, u32[]{:S(2)}) collective-permute-start(bf16[4,1,5,32,256]{4,3,0,2,1:T(8,128)(2,1)} %get-tuple-element.36), channel_id=1, source_target_pairs={{0,1},{1,0},{2,3},{3,2},{4,5},{5,4},{6,7},{7,6},{8,9},{9,8},{10,11... | collective-permute-start | bytes 983048 | tf_op jit(solution)/shard_map/ppermute | solution.py:43
  34.9 50.8 %all-to-all-start = ((bf16[64,8,512]{2,1,0:T(8,128)(2,1)}), bf16[64,8,512]{2,1,0:T(8,128)(2,1)}, u32[]{:S(2)}, u32[]{:S(2)}) async-start(bf16[64,8,512]{2,1,0:T(8,128)(2,1)} %bitcast.2), calls=%async_computation | async-start | bytes 1048576 | tf_op jit(solution)/shard_map/all_to_all | solution.py:80
  52.5 11.6 %collective-permute-start.1 = (bf16[2,2,5,32,256]{4,3,1,2,0:T(8,128)(2,1)S(1)}, bf16[2,2,5,32,256]{4,3,1,2,0:T(8,128)(2,1)S(1)}, u32[]{:S(2)}, u32[]{:S(2)}) collective-permute-start(bf16[2,2,5,32,256]{4,3,1,2,0:T(8,128)(2,1)S(1)} %bitcast.203), channel_id=1, source_target_pairs={{0,2},{1,3},{2,0},{3,1},{4,6},{5,7},{6,4},{7,5},{8,10},{9,11},{10,... | collective-permute-start | bytes 983048 | tf_op jit(solution)/shard_map/ppermute | solution.py:43
  64.2 3.7 %copy-start.9 = (bf16[256,256]{1,0:T(8,128)(2,1)S(1)}, bf16[256,256]{1,0:T(8,128)(2,1)}, u32[]{:S(2)}) copy-start(bf16[256,256]{1,0:T(8,128)(2,1)} %param.13) | copy-start | bytes 393220
  64.3 3.6 %copy-start.13 = (f32[256]{0:T(256)S(1)}, f32[256]{0:T(256)}, u32[]{:S(2)}) copy-start(f32[256]{0:T(256)} %param.10) | copy-start | bytes 3076
  64.3 12.4 %collective-permute-start.2 = (bf16[1,4,5,32,256]{4,3,1,2,0:T(8,128)(2,1)S(1)}, bf16[1,4,5,32,256]{4,3,1,2,0:T(8,128)(2,1)S(1)}, u32[]{:S(2)}, u32[]{:S(2)}) collective-permute-start(bf16[1,4,5,32,256]{4,3,1,2,0:T(8,128)(2,1)S(1)} %get-tuple-element.32), channel_id=1, source_target_pairs={{0,4},{1,5},{2,6},{3,7},{4,0},{5,1},{6,2},{7,3},{8,12},{9,13},{10,... | collective-permute-start | bytes 983048 | tf_op jit(solution)/shard_map/ppermute | solution.py:43
  91.2 0.9 copy-start.6
  91.2 1.0 copy-start.7
  96.3 0.8 copy-start.11
  96.3 0.8 copy-start.12
  96.5 0.7 copy-start.14
  96.5 0.7 copy-start.15
  142.5 0.8 copy-start.4
  143.7 2.4 %copy-start.2 = (f32[3,8,32,256]{3,2,1,0:T(8,128)S(1)}, f32[3,8,32,256]{3,2,1,0:T(8,128)}, u32[]{:S(2)}) copy-start(f32[3,8,32,256]{3,2,1,0:T(8,128)} %get-tuple-element.54) | copy-start | bytes 2359300
  143.7 2.4 %copy-start.5 = (f32[8,32,256]{2,1,0:T(8,128)S(1)}, f32[8,32,256]{2,1,0:T(8,128)}, u32[]{:S(2)}) copy-start(f32[8,32,256]{2,1,0:T(8,128)} %get-tuple-element.49) | copy-start | bytes 786436
  144.4 1.7 %copy-start.10 = (bf16[256,256]{1,0:T(8,128)(2,1)S(1)}, bf16[256,256]{1,0:T(8,128)(2,1)}, u32[]{:S(2)}) copy-start(bf16[256,256]{1,0:T(8,128)(2,1)} %param.13) | copy-start | bytes 393220
